TPU v7x, 256 devices: a whole 4x4x8 slice. The times are simulated.
256 devices in a mesh: req: 64 (over z, x, core), tp: 4 (over y).
Axes of the slice: x: 4, y: 4, z: 8, core: 2. Of those that a mesh axis runs over, the one named last changes fastest.
Arguments:
- hidden: bfloat16 [16384, 2048], P('req'), may hold values from -10.5 to 10.5
- lengths: int32 [64], replicated, may hold values from 1 to 1024, 16384 in all
- dealing: int32 [64], replicated, may hold values from 0 to 63, each once
- norm_gain: bfloat16 [2048], replicated, may hold values from 0.5 to 1.5
- w_query: bfloat16 [2048, 2048], P(None, 'tp'), may hold values from -0.125 to 0.125
- w_key: bfloat16 [2048, 1024], P(None, 'tp'), may hold values from -0.125 to 0.125
- w_value: bfloat16 [2048, 1024], P(None, 'tp'), may hold values from -0.125 to 0.125
- query_gain: bfloat16 [128], replicated, may hold values from 0.5 to 8
- key_gain: bfloat16 [128], replicated, may hold values from 0.5 to 8
- w_out: bfloat16 [2048, 2048], P(None, 'tp'), may hold values from -0.125 to 0.125
Outputs:
- hidden_out: bfloat16 [16384, 2048], P('req', 'tp')
- kv_cache: bfloat16 [2, 64, 1024, 1024], P(None, 'req', None, 'tp')
Inputs may be any that keep to these rules, and one draw needn't show every extreme that they name: The lengths sum to 16384; the largest is exactly 1024. A permutation: dealt slot j, on device j of req, holds prompt dealing[j].
All inputs are finite; a program needn't handle non-finite values.
Results may differ from a plain program's by a relative error of at most 0.012.
The roundings to bfloat16 on the way count: a program that leaves them out, or rounds other values in their place, can miss the bound.
Values may be sent and summed in bfloat16 or wider, within the bound.
No kernel may reach another device: no remote copies, remote signals or barrier semaphores. Data moves between devices by JAX's collectives and lax.ppermute only.
A program may use at most 128 MiB of HBM per device.

v0:
```python
import jax
import jax.numpy as jnp
from jax import lax
from jax.sharding import PartitionSpec as P

EPS = 1e-06
THETA = 1000000.0


def rms_rows(values, scale_gain):
    inv_rms = lax.rsqrt(jnp.mean(values * values, axis=-1, keepdims=True) + EPS)
    return values * inv_rms * scale_gain


def rotate(values, positions):
    features = values.shape[-1]
    half_width = features // 2
    frequency = THETA ** (-(jnp.arange(half_width).astype(jnp.float32) * 2.0) / features)
    angles = positions.astype(jnp.float32)[:, None] * frequency[None, :]
    cosine = jnp.cos(angles)[:, None, :]
    sine_part = jnp.sin(angles)[:, None, :]
    first_half = values[..., :half_width]
    second_half = values[..., half_width:]
    return jnp.concatenate(
        [
            first_half * cosine - second_half * sine_part,
            second_half * cosine + first_half * sine_part,
        ],
        axis=-1,
    )


def project(normed, w_query, w_key, w_value, query_gain, key_gain, positions):
    head_dim = query_gain.shape[0]
    row_count = normed.shape[0]
    query_rows = jnp.dot(normed, w_query, preferred_element_type=jnp.float32).reshape(
        row_count, -1, head_dim
    )
    key_rows = jnp.dot(normed, w_key, preferred_element_type=jnp.float32).reshape(
        row_count, -1, head_dim
    )
    value_rows = jnp.dot(normed, w_value, preferred_element_type=jnp.float32).astype(jnp.bfloat16)
    query_rows = rotate(rms_rows(query_rows, query_gain.astype(jnp.float32)), positions).astype(
        jnp.bfloat16
    )
    key_rows = rotate(rms_rows(key_rows, key_gain.astype(jnp.float32)), positions).astype(
        jnp.bfloat16
    )
    return (query_rows.reshape(row_count, -1), key_rows.reshape(row_count, -1), value_rows)


def attend(query_slot, key_slot, value_slot, prompt_length, head_dim):
    slot_len, query_width = query_slot.shape
    kv_heads = key_slot.shape[1] // head_dim
    group_size = query_width // head_dim // kv_heads
    queries = query_slot.reshape(slot_len, kv_heads, group_size, head_dim)
    keys_split = key_slot.reshape(slot_len, kv_heads, head_dim)
    values_split = value_slot.reshape(slot_len, kv_heads, head_dim)
    scores = jnp.einsum(
        "qkgd,skd->kgqs", queries, keys_split, preferred_element_type=jnp.float32
    ) * head_dim ** (-0.5)
    offsets = jnp.arange(slot_len, dtype=jnp.int32)
    allowed = (offsets[None, :] <= offsets[:, None]) & (offsets[None, :] < prompt_length)
    scores = jnp.where(allowed[None, None], scores, -jnp.inf)
    row_max = jnp.max(scores, axis=-1, keepdims=True)
    weights = jnp.exp(scores - row_max)
    weights = (weights / jnp.sum(weights, axis=-1, keepdims=True)).astype(jnp.bfloat16)
    mixture = jnp.einsum(
        "kgqs,skd->qkgd", weights, values_split, preferred_element_type=jnp.float32
    )
    return mixture.astype(jnp.bfloat16).reshape(slot_len, query_width)


def on_device(
    hidden, lengths, dealing, norm_gain, w_query, w_key, w_value, query_gain, key_gain, w_out
):
    devices = lax.axis_size("req")
    home_index = lax.axis_index("req")
    slice_index = lax.axis_index("tp")
    tok_rows, features = hidden.shape
    head_dim = query_gain.shape[0]
    out_width = w_out.shape[1]
    slot_len = 4 * tok_rows
    capacity = slot_len // devices
    prompt_total = lengths.shape[0]
    prompt_ids = jnp.arange(prompt_total, dtype=jnp.int32)
    prompt_ends = jnp.cumsum(lengths)
    starts = prompt_ends - lengths
    packed_ids = jnp.arange(tok_rows, dtype=jnp.int32) * devices + home_index
    segment = jnp.sum((packed_ids[:, None] >= prompt_ends[None, :]).astype(jnp.int32), axis=1)
    seg_onehot = (segment[:, None] == prompt_ids[None, :]).astype(jnp.int32)
    positions = packed_ids - jnp.sum(seg_onehot * starts[None, :], axis=1)
    inverse = jnp.zeros((prompt_total,), jnp.int32).at[dealing].set(prompt_ids)
    deal_hot = (dealing[:, None] == prompt_ids[None, :]).astype(jnp.int32)
    dealt_starts = jnp.sum(deal_hot * starts[None, :], axis=1)
    dealt_lengths = jnp.sum(deal_hot * lengths[None, :], axis=1)
    first_offset = jnp.mod(home_index - dealt_starts, devices)
    ranks = jnp.arange(capacity, dtype=jnp.int32)
    slot_offset = first_offset[None, :] + ranks[:, None] * devices
    send_valid = slot_offset < dealt_lengths[None, :]
    send_rows = jnp.where(
        send_valid, (dealt_starts[None, :] + slot_offset - home_index) // devices, 0
    ).reshape(-1)
    my_start = lax.dynamic_index_in_dim(dealt_starts, home_index, 0, keepdims=False)
    my_length = lax.dynamic_index_in_dim(dealt_lengths, home_index, 0, keepdims=False)
    roll_shift = jnp.mod(my_start, devices)
    my_slots = jnp.sum(seg_onehot * inverse[None, :], axis=1)
    back_rows = positions // devices * devices + my_slots
    offsets = jnp.arange(slot_len, dtype=jnp.int32)
    gain_values = norm_gain.astype(jnp.float32)
    picked = jnp.take(hidden, send_rows, axis=0).reshape(capacity, devices, hidden.shape[1])
    arrived = lax.all_to_all(
        jnp.where(send_valid[:, :, None], picked, jnp.zeros((), hidden.dtype)),
        "req",
        split_axis=1,
        concat_axis=1,
        tiled=True,
    )
    slot_hidden = jnp.roll(arrived, -roll_shift, axis=1).reshape(slot_len, arrived.shape[2])
    normed = rms_rows(slot_hidden.astype(jnp.float32), gain_values).astype(jnp.bfloat16)
    query_slot, key_slot, value_slot = project(
        normed, w_query, w_key, w_value, query_gain, key_gain, offsets
    )
    mixture = attend(query_slot, key_slot, value_slot, my_length, head_dim)
    sendback = jnp.roll(mixture.reshape(capacity, devices, mixture.shape[1]), roll_shift, axis=1)
    returned = lax.all_to_all(sendback, "req", split_axis=1, concat_axis=1, tiled=True)
    attended = jnp.take(returned.reshape(capacity * devices, -1), back_rows, axis=0)
    kv_cache = jnp.stack([key_slot, value_slot])[:, None]
    summed = jnp.dot(
        lax.all_gather(attended, "tp", axis=1, tiled=True),
        w_out,
        preferred_element_type=jnp.float32,
    )
    branch = lax.optimization_barrier(summed.astype(jnp.bfloat16))
    residual = lax.dynamic_slice_in_dim(hidden, slice_index * out_width, out_width, 1)
    hidden_out = (residual.astype(jnp.float32) + branch.astype(jnp.float32)).astype(jnp.bfloat16)
    return (hidden_out, kv_cache)


def solution(mesh):
    in_specs = (
        P("req", None),
        P(),
        P(),
        P(),
        P(None, "tp"),
        P(None, "tp"),
        P(None, "tp"),
        P(),
        P(),
        P(None, "tp"),
    )
    out_specs = (P("req", "tp"), P(None, "req", None, "tp"))
    return jax.shard_map(
        on_device, mesh=mesh, in_specs=in_specs, out_specs=out_specs, check_vma=False
    )
```

profile of v0, /device:TPU:2, one launch (start us, length us, event | category | flops | bytes accessed | tf_op | source)
XLA Modules:
  0.0 272.4 jit_solution(343829114084428690)
XLA Ops:
  7.2 0.0 copy-start
  7.2 0.9 copy.58
  8.1 0.1 reduce-window.8
  8.2 0.1 reduce.1
  8.3 0.7 sub.85
  9.0 0.8 select_reduce_fusion.2
  9.8 0.7 compare_select_fusion.7
  10.5 0.1 fusion.24
  10.6 0.1 compare_and_fusion
  10.7 0.1 lt.124
  10.7 0.1 copy.59
  10.8 0.1 sub.93
  11.0 0.1 copy.60
  11.1 10.2 %gather_fusion = bf16[1024,2048]{1,0:T(8,128)(2,1)} fusion(bf16[256,2048]{1,0:T(8,128)(2,1)} %param.10, s32[1024]{0:T(1024)S(1)} %broadcast_clamp_fusion), kind=kCustom, calls=%fused_computation | custom fusion | bytes 8392704 | tf_op jit(solution)/shard_map/jit(_take)/gather | solution.py:111
  21.3 9.6 %fusion.10 = bf16[16,64,2048]{2,0,1:T(8,128)(2,1)} fusion(bf16[16,64,2048]{2,1,0:T(8,128)(2,1)} %bitcast.70, pred[16,64]{0,1:T(8,128)(4,1)S(1)} %copy.60, pred[16,64]{0,1:T(8,128)(4,1)S(1)} %copy.59), kind=kLoop, calls=%fused_computation.22 | loop fusion | flops 4194304 | bytes 8390656 | tf_op jit(solution)/shard_map/jit(_where)/select_n | solution.py:113
  30.9 12.3 %all-to-all-start = ((bf16[16,64,2048]{2,0,1:T(8,128)(2,1)}), bf16[16,64,2048]{2,0,1:T(8,128)(2,1)}, u32[]{:S(2)}, u32[]{:S(2)}) async-start(bf16[16,64,2048]{2,0,1:T(8,128)(2,1)} %fusion.10), calls=%async_computation | async-start | bytes 8388608 | tf_op jit(solution)/shard_map/all_to_all | solution.py:112
  43.2 0.0 copy-start.6
  43.3 0.6 dynamic_slice.19
  45.8 0.6 dynamic_slice.21
  46.4 4.0 %copy.80 = bf16[512,2048]{1,0:T(8,128)(2,1)} copy(bf16[512,2048]{0,1:T(8,128)(2,1)} %bitcast.76) | data formatting | bytes 4194304 | tf_op jit(solution)/shard_map/dot_general | solution.py:36
  50.4 1.4 copy.77
  51.9 0.7 iota_compare_fusion.3
  52.5 1.0 multiply_cosine_fusion
  53.5 1.3 fusion.11
  54.9 84.4 %all-to-all-done = bf16[16,64,2048]{2,0,1:T(8,128)(2,1)} async-done(((bf16[16,64,2048]{2,0,1:T(8,128)(2,1)}), bf16[16,64,2048]{2,0,1:T(8,128)(2,1)}, u32[]{:S(2)}, u32[]{:S(2)}) %all-to-all-start) | async-done | bytes 4194336 | tf_op jit(solution)/shard_map/all_to_all | solution.py:112
  139.3 4.5 %copy.62 = bf16[16,64,2048]{2,1,0:T(8,128)(2,1)S(1)} copy(bf16[16,64,2048]{2,0,1:T(8,128)(2,1)} %all-to-all-done) | data formatting | bytes 8388608 | tf_op jit(solution)/shard_map/all_to_all | solution.py:112
  143.8 6.5 %multiply_reduce_fusion = (f32[16,64]{1,0:T(8,128)S(1)}, f32[16,64,2048]{2,1,0:T(8,128)}) fusion(s32[]{:T(128)S(6)} %select_n.166, bf16[16,64,2048]{2,1,0:T(8,128)(2,1)S(1)} %copy.62), kind=kLoop, calls=%fused_computation.16 | loop fusion | flops 12581888 | bytes 12587012 | tf_op jit(solution)/shard_map/reduce_sum | solution.py:11
  150.3 0.1 rsqrt.29
  150.3 4.3 %multiply_convert_fusion = bf16[16,64,2048]{2,1,0:T(8,128)(2,1)S(1)} fusion(f32[16,64,2048]{2,1,0:T(8,128)} %get-tuple-element.17, f32[2048]{0:T(1024)S(1)} %convert_element_type.122, f32[16,64]{1,0:T(8,128)S(1)} %add_rsqrt_fusion.2), kind=kLoop, calls=%fused_computation.15 | loop fusion | flops 6291456 | bytes 12595200 | tf_op jit(solution)/shard_map/convert_element_type | solution.py:120
  154.6 1.5 copy-done.1
  156.1 2.7 fusion.3
  158.8 0.7 copy-done.3
  159.5 2.4 multiply_reduce_fusion.1
  162.0 0.5 multiply_multiply_fusion
  162.4 1.2 subtract_convert_fusion
  163.6 2.4 copy.67
  166.0 1.4 copy.66
  167.4 3.9 %multiply_reduce_fusion.2 = (f32[1024,2]{0,1:T(2,128)S(1)}, f32[1024,2,128]{0,2,1:T(8,128)S(1)}) fusion(bf16[1024,2048,1]{1,0,2:T(8,128)(2,1)} %bitcast.73, bf16[2,128,2048]{2,1,0:T(8,128)(2,1)} %bitcast.80), kind=kOutput, calls=%fused_computation.41 | convolution fusion | flops 1074264064 | bytes 6299648 | tf_op jit(solution)/shard_map/dot_general | solution.py:39
  171.3 0.2 multiply_multiply_fusion.1
  171.5 0.9 multiply_subtract_fusion
  172.4 1.2 copy-done.2
  173.6 2.1 convolution_convert_fusion
  175.7 11.5 %fusion.38 = (f32[2,2,1024]{2,1,0:T(2,128)S(1)}, f32[2,2,1024,1024]{2,3,1,0:T(8,128)}) fusion(pred[1024,1024]{0,1:T(8,128)(4,1)S(1)} %copy-done.5, bf16[1024,2,2,64]{3,0,2,1:T(8,128)(2,1)} %copy.67, bf16[1024,2,2,64]{3,0,2,1:T(8,128)(2,1)} %copy.66, bf16[1024,2,64]{0,2,1:T(8,128)(2,1)} %get-tuple-element.21, bf16[1024,2,64]{0,2,1:T(8,128)(2,1)S(1)} %get-tuple-element.20), kind=kOutput, calls=%fused_computation.108 | convolution fusion | flops 1093665792 | bytes 19415040 | tf_op jit(solution)/shard_map/sub | solution.py:66
  187.1 7.2 %fusion.15 = bf16[1024,2,2,128]{0,3,2,1:T(8,128)(2,1)S(1)} fusion(bf16[1024,2,128,1]{0,2,3,1:T(8,128)(2,1)} %bitcast.81, f32[2,2,1024,1024]{2,3,1,0:T(8,128)} %get-tuple-element.31, f32[2,2,1024]{2,1,0:T(2,128)S(1)} %get-tuple-element.30), kind=kOutput, calls=%fused_computation.31 | convolution fusion | flops 1082654720 | bytes 18366464 | tf_op jit(solution)/shard_map/kgqs,skd->qkgd/dot_general | solution.py:68
  194.4 2.0 copy.70
  196.4 1.5 reshape_reshape.4
  197.9 0.8 fusion.16
  198.7 1.5 copy.71
  200.3 5.6 %all-to-all-start.1 = ((bf16[16,64,512]{2,0,1:T(8,128)(2,1)}), bf16[16,64,512]{2,0,1:T(8,128)(2,1)}, u32[]{:S(2)}, u32[]{:S(2)}) async-start(bf16[16,64,512]{2,0,1:T(8,128)(2,1)} %copy.71), calls=%async_computation.1 | async-start | bytes 2097152 | tf_op jit(solution)/shard_map/all_to_all | solution.py:126
  205.9 0.0 all-gather.2.cloned.1.call-start
  206.0 0.8 scatter_custom_fusion
  206.7 0.1 convert_reduce_fusion
  206.8 0.1 select_reduce_fusion.1
  207.0 27.6 %all-to-all-done.1 = bf16[16,64,512]{2,0,1:T(8,128)(2,1)} async-done(((bf16[16,64,512]{2,0,1:T(8,128)(2,1)}), bf16[16,64,512]{2,0,1:T(8,128)(2,1)}, u32[]{:S(2)}, u32[]{:S(2)}) %all-to-all-start.1) | async-done | bytes 1048608 | tf_op jit(solution)/shard_map/all_to_all | solution.py:126
  234.6 1.8 copy.72
  236.5 1.2 gather_fusion.1
  237.6 0.8 broadcast_select_fusion
  238.4 0.0 all-gather.2.cloned.1.call-update
  238.5 1.1 maximum_convert_fusion
  239.5 1.1 maximum_bitcast_fusion
  240.7 1.3 copy.73
  242.0 20.0 %all-gather.2.cloned.1.call-done = bf16[256,2048]{1,0:T(8,128)(2,1)} async-done(((bf16[256,512]{1,0:T(8,128)(2,1)}), bf16[256,2048]{1,0:T(8,128)(2,1)}) %all-gather.2.cloned.1.call-update) | async-done | bytes 1048592 | tf_op jit(solution)/shard_map/all_gather | solution.py:130
  261.9 1.9 convolution_convert_fusion.1
  263.9 1.7 add_convert_fusion.1
  (35 shorter events, 0.2 us)
Async XLA Ops:
  7.2 254.8 %copy-start = (bf16[2048,512]{1,0:T(8,128)(2,1)S(1)}, bf16[2048,512]{1,0:T(8,128)(2,1)}, u32[]{:S(2)}) copy-start(bf16[2048,512]{1,0:T(8,128)(2,1)} %param.19) | copy-start | bytes 6291460
  30.9 15.6 %copy-start.8 = (bf16[2048]{0:T(1024)(128)(2,1)S(1)}, bf16[2048]{0:T(1024)(128)(2,1)}, u32[]{:S(2)}) copy-start(bf16[2048]{0:T(1024)(128)(2,1)} %param.13) | copy-start | bytes 12292
  30.9 108.4 %all-to-all-start = ((bf16[16,64,2048]{2,0,1:T(8,128)(2,1)}), bf16[16,64,2048]{2,0,1:T(8,128)(2,1)}, u32[]{:S(2)}, u32[]{:S(2)}) async-start(bf16[16,64,2048]{2,0,1:T(8,128)(2,1)} %fusion.10), calls=%async_computation | async-start | bytes 8388608 | tf_op jit(solution)/shard_map/all_to_all | solution.py:112
  43.2 7.2 %copy-start.10 = (bf16[128]{0:T(256)(128)(2,1)S(1)}, bf16[128]{0:T(256)(128)(2,1)}, u32[]{:S(2)}) copy-start(bf16[128]{0:T(256)(128)(2,1)} %param.17) | copy-start | bytes 772
  43.2 7.2 %copy-start.6 = (bf16[2048,256]{1,0:T(8,128)(2,1)S(1)}, bf16[2048,256]{1,0:T(8,128)(2,1)}, u32[]{:S(2)}) copy-start(bf16[2048,256]{1,0:T(8,128)(2,1)} %param.15) | copy-start | bytes 3145732
  43.2 8.6 %copy-start.11 = (bf16[128]{0:T(256)(128)(2,1)S(1)}, bf16[128]{0:T(256)(128)(2,1)}, u32[]{:S(2)}) copy-start(bf16[128]{0:T(256)(128)(2,1)} %param.18) | copy-start | bytes 772
  150.3 5.8 %copy-start.1 = (f32[16,64,2048]{2,1,0:T(8,128)S(1)}, f32[16,64,2048]{2,1,0:T(8,128)}, u32[]{:S(2)}) copy-start(f32[16,64,2048]{2,1,0:T(8,128)} %get-tuple-element.17) | copy-start | bytes 25165828
  156.1 3.4 %copy-start.3 = (bf16[16,64,2048]{2,1,0:T(8,128)(2,1)}, bf16[16,64,2048]{2,1,0:T(8,128)(2,1)S(1)}, u32[]{:S(2)}) copy-start(bf16[16,64,2048]{2,1,0:T(8,128)(2,1)S(1)} %multiply_convert_fusion) | copy-start | bytes 12582916
  156.1 3.4 %copy-start.4 = (bf16[512,2048]{1,0:T(8,128)(2,1)S(1)}, bf16[512,2048]{1,0:T(8,128)(2,1)}, u32[]{:S(2)}) copy-start(bf16[512,2048]{1,0:T(8,128)(2,1)} %copy.80) | copy-start | bytes 6291460
  167.4 5.0 %copy-start.9 = (bf16[2048,256]{1,0:T(8,128)(2,1)S(1)}, bf16[2048,256]{1,0:T(8,128)(2,1)}, u32[]{:S(2)}) copy-start(bf16[2048,256]{1,0:T(8,128)(2,1)} %param.16) | copy-start | bytes 3145732
  171.3 2.3 copy-start.2
  173.6 2.1 copy-start.7
  173.6 2.1 copy-start.5
  200.3 34.4 %all-to-all-start.1 = ((bf16[16,64,512]{2,0,1:T(8,128)(2,1)}), bf16[16,64,512]{2,0,1:T(8,128)(2,1)}, u32[]{:S(2)}, u32[]{:S(2)}) async-start(bf16[16,64,512]{2,0,1:T(8,128)(2,1)} %copy.71), calls=%async_computation.1 | async-start | bytes 2097152 | tf_op jit(solution)/shard_map/all_to_all | solution.py:126
  205.9 56.0 %all-gather.2.cloned.1.call-start = ((), (), s32[]{:S(2)}) async-start(), calls=%async_computation.2 | async-start | bytes 1310720 | tf_op jit(solution)/shard_map/all_gather | solution.py:130
Sparse Core Ops, SparseCore 0:
  238.6 23.3 all-gather.1
where the time goes:
time: 273 us; the launch traced here: 272 us
  waiting for transfers between devices  132 us (48%)
  local copies, waits for them, and re-layouts  39.9 us (15%)
  other arithmetic  37.2 us (14%)
  matrix products  29 us (11%)
  starting transfers between devices  18 us (7%)
  between operations  16.3 us (6%)
    all_to_all x1, waiting for transfers between devices, on_device(): lax.all_to_all(jnp.where(send_valid[:, :, None], picked, jnp.zeros((), hi...  84.4 us
    all_to_all x1, waiting for transfers between devices, on_device(): lax.all_to_all(sendback, 'req', split_axis=1, concat_axis=1, tiled=True)  27.6 us
    all_gather x1, waiting for transfers between devices, on_device(): lax.all_gather(attended, 'tp', axis=1, tiled=True)  20 us
    all_to_all x1, starting transfers between devices, on_device(): lax.all_to_all(jnp.where(send_valid[:, :, None], picked, jnp.zeros((), hi...  12.3 us
    sub x1, matrix products, attend(): weights = jnp.exp(scores - row_max)  11.5 us
    gather x1, local copies, waits for them, and re-layouts, on_device(): jnp.take(hidden, send_rows, axis=0)  10.2 us
    select_n x1, other arithmetic, on_device(): jnp.where(send_valid[:, :, None], picked, jnp.zeros((), hidden.dtype))  9.61 us
    dot_general x1, matrix products, attend(): jnp.einsum('kgqs,skd->qkgd', weights, values_split, preferred_element_typ...  7.24 us
  transfers between devices with their start and end apart: 3, of which 3 were waited for; matrix products, arithmetic and copies ran while one was open for 5% of the time, Pallas kernels for 0%

commit v1 on v0

--- a/solution.py
+++ b/solution.py
@@ -1,10 +1,44 @@
+import functools
 import jax
 import jax.numpy as jnp
 from jax import lax
 from jax.sharding import PartitionSpec as P
+from jax.lax import axis_index, axis_size, ppermute
 
 EPS = 1e-06
 THETA = 1000000.0
+
+
+def mark_pieces_all_on_mesh(arr, dim_at):
+    heard = list(arr.shape[1:])
+    heard[dim_at] *= arr.shape[0]
+    return jnp.moveaxis(arr, 0, dim_at).reshape(heard)
+
+
+def close_counts_now(content, axis_tag, at_axis):
+    n_shards = axis_size(axis_tag)
+    runs = []
+    for h in range(n_shards):
+        runs.append((h, (h + 1) % n_shards))
+    pile = []
+    for dd, t in runs:
+        pile.append((t, dd))
+    vec_out, s_next = ([], [])
+    for pp in range(n_shards - 1):
+        if pp % 2 == 0:
+            mid_arr = ppermute(vec_out[-1] if vec_out else content, axis_tag, runs)
+            vec_out.append(mid_arr)
+        else:
+            outcome_arr = ppermute(s_next[-1] if s_next else content, axis_tag, pile)
+            s_next.append(outcome_arr)
+    e_next = jnp.stack([*vec_out[::-1], content, *s_next], axis=0)
+    b_next = axis_index(axis_tag)
+    long_array = b_next - len(vec_out)
+    e_next = e_next[(jnp.arange(n_shards) - long_array) % n_shards]
+    return mark_pieces_all_on_mesh(e_next, at_axis)
+
+
+see_indices = functools.partial(close_counts_now, axis_tag="tp", at_axis=1)
 
 
 def rms_rows(values, scale_gain):
@@ -126,11 +160,7 @@
     returned = lax.all_to_all(sendback, "req", split_axis=1, concat_axis=1, tiled=True)
     attended = jnp.take(returned.reshape(capacity * devices, -1), back_rows, axis=0)
     kv_cache = jnp.stack([key_slot, value_slot])[:, None]
-    summed = jnp.dot(
-        lax.all_gather(attended, "tp", axis=1, tiled=True),
-        w_out,
-        preferred_element_type=jnp.float32,
-    )
+    summed = jnp.dot(see_indices(attended), w_out, preferred_element_type=jnp.float32)
     branch = lax.optimization_barrier(summed.astype(jnp.bfloat16))
     residual = lax.dynamic_slice_in_dim(hidden, slice_index * out_width, out_width, 1)
     hidden_out = (residual.astype(jnp.float32) + branch.astype(jnp.float32)).astype(jnp.bfloat16)

time: 273 us -> 257 us (0.941)
  between operations: 16.3 us -> 2.94 us
  waiting for transfers between devices: 132 us -> 121 us
  starting transfers between devices: 18 us -> 21.6 us
  local copies, waits for them, and re-layouts: 39.9 us -> 42.9 us
    all_gather x1 -> x0, waiting for transfers between devices: 20 us -> none  [on_device(): lax.all_gather(attended, 'tp', axis=1, tiled=True)]
    ppermute x0 -> x3, waiting for transfers between devices: none -> 9.28 us  [the longest x2 9.28 us: close_counts_now(): mid_arr = ppermute(vec_out[-1] if vec_out else content, axis_tag, runs)]
    ppermute x0 -> x3, starting transfers between devices: none -> 3.62 us  [the longest x2 1.88 us: close_counts_now(): mid_arr = ppermute(vec_out[-1] if vec_out else content, axis_tag, runs)]
  transfers between devices with their start and end apart: 3 -> 5, of which waited for: 3 -> 4; matrix products, arithmetic and copies ran while one was open for 5% -> 6% of each run, Pallas kernels for 0% -> 0%
where the time goes in v1:
time: 257 us; the launch traced here: 255 us
  waiting for transfers between devices  121 us (47%)
  local copies, waits for them, and re-layouts  42.9 us (17%)
  other arithmetic  38.6 us (15%)
  matrix products  27.8 us (11%)
  starting transfers between devices  21.6 us (8%)
  between operations  2.94 us (1%)
    all_to_all x1, waiting for transfers between devices, on_device(): lax.all_to_all(jnp.where(send_valid[:, :, None], picked, jnp.zeros((), hi...  84.4 us
    all_to_all x1, waiting for transfers between devices, on_device(): lax.all_to_all(sendback, 'req', split_axis=1, concat_axis=1, tiled=True)  27.7 us
    all_to_all x1, starting transfers between devices, on_device(): lax.all_to_all(jnp.where(send_valid[:, :, None], picked, jnp.zeros((), hi...  12.3 us
    sub x1, matrix products, attend(): weights = jnp.exp(scores - row_max)  11.5 us
    gather x1, local copies, waits for them, and re-layouts, on_device(): jnp.take(hidden, send_rows, axis=0)  10.2 us
    select_n x1, other arithmetic, on_device(): jnp.where(send_valid[:, :, None], picked, jnp.zeros((), hidden.dtype))  9.61 us
    ppermute x2, waiting for transfers between devices, close_counts_now(): mid_arr = ppermute(vec_out[-1] if vec_out else content, axis_tag, runs)  9.28 us
    dot_general x1, matrix products, attend(): jnp.einsum('kgqs,skd->qkgd', weights, values_split, preferred_element_typ...  7.24 us
  transfers between devices with their start and end apart: 5, of which 4 were waited for; matrix products, arithmetic and copies ran while one was open for 6% of the time, Pallas kernels for 0%

profile of v1, /device:TPU:2, one launch (start us, length us, event | category | flops | bytes accessed | tf_op | source)
XLA Modules:
  0.0 255.2 jit_solution(5002934812355951578)
XLA Ops:
  0.7 0.9 copy.61
  1.6 0.1 reduce-window.8
  1.6 0.1 reduce.1
  1.8 0.7 sub.101
  2.4 0.8 select_reduce_fusion.2
  3.3 0.7 compare_select_fusion.8
  4.0 0.1 compare_and_fusion
  4.2 0.1 copy.62
  4.4 0.1 copy.63
  4.5 10.2 %gather_fusion = bf16[1024,2048]{1,0:T(8,128)(2,1)} fusion(bf16[256,2048]{1,0:T(8,128)(2,1)} %param.10, s32[1024]{0:T(1024)S(1)} %broadcast_clamp_fusion), kind=kCustom, calls=%fused_computation | custom fusion | bytes 8392704 | tf_op jit(solution)/shard_map/jit(_take)/gather | solution.py:145
  14.7 9.6 %fusion.10 = bf16[16,64,2048]{2,0,1:T(8,128)(2,1)} fusion(bf16[16,64,2048]{2,1,0:T(8,128)(2,1)} %bitcast.79, pred[16,64]{0,1:T(8,128)(4,1)S(1)} %copy.63, pred[16,64]{0,1:T(8,128)(4,1)S(1)} %copy.62), kind=kLoop, calls=%fused_computation.23 | loop fusion | flops 4194304 | bytes 8390656 | tf_op jit(solution)/shard_map/jit(_where)/select_n | solution.py:147
  24.3 12.3 %all-to-all-start = ((bf16[16,64,2048]{2,0,1:T(8,128)(2,1)}), bf16[16,64,2048]{2,0,1:T(8,128)(2,1)}, u32[]{:S(2)}, u32[]{:S(2)}) async-start(bf16[16,64,2048]{2,0,1:T(8,128)(2,1)} %fusion.10), calls=%async_computation | async-start | bytes 8388608 | tf_op jit(solution)/shard_map/all_to_all | solution.py:146
  36.7 0.6 dynamic_slice.19
  39.3 0.6 dynamic_slice.21
  39.9 4.0 %copy.84 = bf16[512,2048]{1,0:T(8,128)(2,1)} copy(bf16[512,2048]{0,1:T(8,128)(2,1)} %bitcast.86) | data formatting | bytes 4194304 | tf_op jit(solution)/shard_map/dot_general | solution.py:70
  43.9 1.4 copy.81
  45.3 0.7 iota_compare_fusion.3
  46.0 1.0 multiply_cosine_fusion
  47.0 1.3 fusion.11
  48.3 84.4 %all-to-all-done = bf16[16,64,2048]{2,0,1:T(8,128)(2,1)} async-done(((bf16[16,64,2048]{2,0,1:T(8,128)(2,1)}), bf16[16,64,2048]{2,0,1:T(8,128)(2,1)}, u32[]{:S(2)}, u32[]{:S(2)}) %all-to-all-start) | async-done | bytes 4194336 | tf_op jit(solution)/shard_map/all_to_all | solution.py:146
  132.8 4.5 %copy.65 = bf16[16,64,2048]{2,1,0:T(8,128)(2,1)S(1)} copy(bf16[16,64,2048]{2,0,1:T(8,128)(2,1)} %all-to-all-done) | data formatting | bytes 8388608 | tf_op jit(solution)/shard_map/all_to_all | solution.py:146
  137.3 6.5 %multiply_reduce_fusion = (f32[16,64]{1,0:T(8,128)S(1)}, f32[16,64,2048]{2,1,0:T(8,128)}) fusion(s32[]{:T(128)S(6)} %select_n.198, bf16[16,64,2048]{2,1,0:T(8,128)(2,1)S(1)} %copy.65), kind=kLoop, calls=%fused_computation.17 | loop fusion | flops 12581888 | bytes 12587012 | tf_op jit(solution)/shard_map/reduce_sum | solution.py:45
  143.8 4.3 %multiply_convert_fusion = bf16[16,64,2048]{2,1,0:T(8,128)(2,1)S(1)} fusion(f32[16,64,2048]{2,1,0:T(8,128)} %get-tuple-element.17, f32[2048]{0:T(1024)S(1)} %convert_element_type.122, f32[16,64]{1,0:T(8,128)S(1)} %add_rsqrt_fusion.2), kind=kLoop, calls=%fused_computation.16 | loop fusion | flops 6291456 | bytes 12595200 | tf_op jit(solution)/shard_map/convert_element_type | solution.py:154
  148.1 1.5 copy-done.1
  149.6 2.7 %fusion.3 = bf16[1024,2048]{1,0:T(8,128)(2,1)} fusion(f32[16,64,2048]{2,1,0:T(8,128)S(1)} %copy-done.1, f32[2048]{0:T(1024)S(1)} %convert_element_type.122, f32[1024]{0:T(1024)S(1)} %rsqrt.29), kind=kLoop, calls=%fused_computation.13 | loop fusion | flops 6291456 | bytes 12595200 | tf_op jit(solution)/shard_map/convert_element_type | solution.py:154
  152.3 0.7 copy-done.3
  153.0 2.4 multiply_reduce_fusion.1
  155.4 0.5 multiply_multiply_fusion
  155.9 1.2 subtract_convert_fusion
  157.1 2.4 copy.70
  159.5 1.4 copy.69
  160.9 3.9 %multiply_reduce_fusion.2 = (f32[1024,2]{0,1:T(2,128)S(1)}, f32[1024,2,128]{0,2,1:T(8,128)S(1)}) fusion(bf16[1024,2048,1]{1,0,2:T(8,128)(2,1)} %bitcast.83, bf16[2,128,2048]{2,1,0:T(8,128)(2,1)} %bitcast.90), kind=kOutput, calls=%fused_computation.43 | convolution fusion | flops 1074264064 | bytes 6299648 | tf_op jit(solution)/shard_map/dot_general | solution.py:73
  164.8 0.2 multiply_multiply_fusion.1
  165.0 0.9 multiply_subtract_fusion
  165.9 1.2 copy-done.2
  167.0 2.1 convolution_convert_fusion
  169.1 11.5 %fusion.40 = (f32[2,2,1024]{2,1,0:T(2,128)S(1)}, f32[2,2,1024,1024]{2,3,1,0:T(8,128)}) fusion(pred[1024,1024]{0,1:T(8,128)(4,1)S(1)} %copy-done.5, bf16[1024,2,2,64]{3,0,2,1:T(8,128)(2,1)} %copy.70, bf16[1024,2,2,64]{3,0,2,1:T(8,128)(2,1)} %copy.69, bf16[1024,2,64]{0,2,1:T(8,128)(2,1)} %get-tuple-element.21, bf16[1024,2,64]{0,2,1:T(8,128)(2,1)S(1)} %get-tuple-element.20), kind=kOutput, calls=%fused_computation.118 | convolution fusion | flops 1093665792 | bytes 19415040 | tf_op jit(solution)/shard_map/sub | solution.py:100
  180.6 7.2 %fusion.15 = bf16[1024,2,2,128]{0,3,2,1:T(8,128)(2,1)S(1)} fusion(bf16[1024,2,128,1]{0,2,3,1:T(8,128)(2,1)} %bitcast.92, f32[2,2,1024,1024]{2,3,1,0:T(8,128)} %get-tuple-element.31, f32[2,2,1024]{2,1,0:T(2,128)S(1)} %get-tuple-element.30), kind=kOutput, calls=%fused_computation.32 | convolution fusion | flops 1082654720 | bytes 18366464 | tf_op jit(solution)/shard_map/kgqs,skd->qkgd/dot_general | solution.py:102
  187.9 2.0 copy.73
  189.9 1.5 reshape_reshape.4
  191.4 0.8 fusion.16
  192.2 1.5 copy.74
  193.7 5.6 %all-to-all-start.1 = ((bf16[16,64,512]{2,0,1:T(8,128)(2,1)}), bf16[16,64,512]{2,0,1:T(8,128)(2,1)}, u32[]{:S(2)}, u32[]{:S(2)}) async-start(bf16[16,64,512]{2,0,1:T(8,128)(2,1)} %copy.74), calls=%async_computation.1 | async-start | bytes 2097152 | tf_op jit(solution)/shard_map/all_to_all | solution.py:160
  199.4 0.8 scatter_custom_fusion
  200.2 0.1 convert_reduce_fusion
  200.3 0.1 select_reduce_fusion.1
  200.4 27.7 %all-to-all-done.1 = bf16[16,64,512]{2,0,1:T(8,128)(2,1)} async-done(((bf16[16,64,512]{2,0,1:T(8,128)(2,1)}), bf16[16,64,512]{2,0,1:T(8,128)(2,1)}, u32[]{:S(2)}, u32[]{:S(2)}) %all-to-all-start.1) | async-done | bytes 1048608 | tf_op jit(solution)/shard_map/all_to_all | solution.py:160
  228.1 1.8 copy.75
  229.9 1.2 gather_fusion.1
  231.1 0.8 broadcast_select_fusion
  231.9 1.6 collective-permute-start
  233.5 1.1 maximum_convert_fusion
  234.5 1.7 collective-permute-start.2
  236.3 4.3 %collective-permute-done = bf16[256,512]{1,0:T(8,128)(2,1)} collective-permute-done((bf16[256,512]{1,0:T(8,128)(2,1)}, bf16[256,512]{1,0:T(8,128)(2,1)}, u32[]{:S(2)}, u32[]{:S(2)}) %collective-permute-start) | collective-permute-done | bytes 262176 | tf_op jit(solution)/shard_map/ppermute | solution.py:29
  240.5 0.3 collective-permute-start.1
  240.8 1.1 maximum_bitcast_fusion
  242.0 1.3 copy.77
  243.3 0.1 bitcast_select_fusion.4
  243.4 5.0 %collective-permute-done.1 = bf16[256,512]{1,0:T(8,128)(2,1)} collective-permute-done((bf16[256,512]{1,0:T(8,128)(2,1)}, bf16[256,512]{1,0:T(8,128)(2,1)}, u32[]{:S(2)}, u32[]{:S(2)}) %collective-permute-start.1) | collective-permute-done | bytes 262176 | tf_op jit(solution)/shard_map/ppermute | solution.py:29
  248.4 1.2 pad_maximum_fusion.1
  249.7 1.6 gather_fusion.2
  251.3 1.5 copy.76
  252.8 0.7 convolution_convert_fusion.1
  253.5 1.7 add_convert_fusion.1
  (44 shorter events, 0.5 us)
Async XLA Ops:
  0.6 252.1 %copy-start = (bf16[2048,512]{1,0:T(8,128)(2,1)S(1)}, bf16[2048,512]{1,0:T(8,128)(2,1)}, u32[]{:S(2)}) copy-start(bf16[2048,512]{1,0:T(8,128)(2,1)} %param.19) | copy-start | bytes 6291460
  24.3 15.6 %copy-start.8 = (bf16[2048]{0:T(1024)(128)(2,1)S(1)}, bf16[2048]{0:T(1024)(128)(2,1)}, u32[]{:S(2)}) copy-start(bf16[2048]{0:T(1024)(128)(2,1)} %param.13) | copy-start | bytes 12292
  24.3 108.4 %all-to-all-start = ((bf16[16,64,2048]{2,0,1:T(8,128)(2,1)}), bf16[16,64,2048]{2,0,1:T(8,128)(2,1)}, u32[]{:S(2)}, u32[]{:S(2)}) async-start(bf16[16,64,2048]{2,0,1:T(8,128)(2,1)} %fusion.10), calls=%async_computation | async-start | bytes 8388608 | tf_op jit(solution)/shard_map/all_to_all | solution.py:146
  36.7 7.2 %copy-start.10 = (bf16[128]{0:T(256)(128)(2,1)S(1)}, bf16[128]{0:T(256)(128)(2,1)}, u32[]{:S(2)}) copy-start(bf16[128]{0:T(256)(128)(2,1)} %param.17) | copy-start | bytes 772
  36.7 7.2 %copy-start.6 = (bf16[2048,256]{1,0:T(8,128)(2,1)S(1)}, bf16[2048,256]{1,0:T(8,128)(2,1)}, u32[]{:S(2)}) copy-start(bf16[2048,256]{1,0:T(8,128)(2,1)} %param.15) | copy-start | bytes 3145732
  36.7 8.6 %copy-start.11 = (bf16[128]{0:T(256)(128)(2,1)S(1)}, bf16[128]{0:T(256)(128)(2,1)}, u32[]{:S(2)}) copy-start(bf16[128]{0:T(256)(128)(2,1)} %param.18) | copy-start | bytes 772
  143.8 5.8 %copy-start.1 = (f32[16,64,2048]{2,1,0:T(8,128)S(1)}, f32[16,64,2048]{2,1,0:T(8,128)}, u32[]{:S(2)}) copy-start(f32[16,64,2048]{2,1,0:T(8,128)} %get-tuple-element.17) | copy-start | bytes 25165828
  149.6 3.4 %copy-start.3 = (bf16[16,64,2048]{2,1,0:T(8,128)(2,1)}, bf16[16,64,2048]{2,1,0:T(8,128)(2,1)S(1)}, u32[]{:S(2)}) copy-start(bf16[16,64,2048]{2,1,0:T(8,128)(2,1)S(1)} %multiply_convert_fusion) | copy-start | bytes 12582916
  149.6 3.4 %copy-start.4 = (bf16[512,2048]{1,0:T(8,128)(2,1)S(1)}, bf16[512,2048]{1,0:T(8,128)(2,1)}, u32[]{:S(2)}) copy-start(bf16[512,2048]{1,0:T(8,128)(2,1)} %copy.84) | copy-start | bytes 6291460
  160.9 5.0 %copy-start.9 = (bf16[2048,256]{1,0:T(8,128)(2,1)S(1)}, bf16[2048,256]{1,0:T(8,128)(2,1)}, u32[]{:S(2)}) copy-start(bf16[2048,256]{1,0:T(8,128)(2,1)} %param.16) | copy-start | bytes 3145732
  164.8 2.3 copy-start.2
  167.0 2.1 copy-start.7
  167.0 2.1 copy-start.5
  193.7 34.4 %all-to-all-start.1 = ((bf16[16,64,512]{2,0,1:T(8,128)(2,1)}), bf16[16,64,512]{2,0,1:T(8,128)(2,1)}, u32[]{:S(2)}, u32[]{:S(2)}) async-start(bf16[16,64,512]{2,0,1:T(8,128)(2,1)} %copy.74), calls=%async_computation.1 | async-start | bytes 2097152 | tf_op jit(solution)/shard_map/all_to_all | solution.py:160
  231.9 8.7 %collective-permute-start = (bf16[256,512]{1,0:T(8,128)(2,1)}, bf16[256,512]{1,0:T(8,128)(2,1)}, u32[]{:S(2)}, u32[]{:S(2)}) collective-permute-start(bf16[256,512]{1,0:T(8,128)(2,1)} %broadcast_select_fusion), channel_id=1, source_target_pairs={{0,1},{1,2},{2,3},{3,0},{4,5},{5,6},{6,7},{7,4},{8,9},{9,10},{10,1... | collective-permute-start | bytes 786440 | tf_op jit(solution)/shard_map/ppermute | solution.py:29
  234.5 8.9 %collective-permute-start.2 = (bf16[256,512]{1,0:T(8,128)(2,1)}, bf16[256,512]{1,0:T(8,128)(2,1)}, u32[]{:S(2)}, u32[]{:S(2)}) collective-permute-start(bf16[256,512]{1,0:T(8,128)(2,1)} %broadcast_select_fusion), channel_id=1, source_target_pairs={{1,0},{2,1},{3,2},{0,3},{5,4},{6,5},{7,6},{4,7},{9,8},{10,9},{11,1... | collective-permute-start | bytes 786440 | tf_op jit(solution)/shard_map/ppermute | solution.py:32
  240.5 7.9 %collective-permute-start.1 = (bf16[256,512]{1,0:T(8,128)(2,1)}, bf16[256,512]{1,0:T(8,128)(2,1)}, u32[]{:S(2)}, u32[]{:S(2)}) collective-permute-start(bf16[256,512]{1,0:T(8,128)(2,1)} %collective-permute-done), channel_id=1, source_target_pairs={{0,1},{1,2},{2,3},{3,0},{4,5},{5,6},{6,7},{7,4},{8,9},{9,10},{10,1... | collective-permute-start | bytes 786440 | tf_op jit(solution)/shard_map/ppermute | solution.py:29
